TPU v7x, 32 devices: a whole 2x2x4 slice. The times are simulated.
32 devices in a mesh: groups: 2 (over y), ctx: 4 (over z), head: 4 (over x, core).
Axes of the slice: x: 2, y: 2, z: 4, core: 2. Of those that a mesh axis runs over, the one named last changes fastest.
Arguments:
- queries: bfloat16 [8192, 512], P(('groups', 'ctx', 'head')), parts along dimension 0, may hold values from -8 to 8, as said below
- keys: bfloat16 [8192, 512], P(('groups', 'ctx', 'head')), parts along dimension 0, may hold values from -8 to 8
- values: bfloat16 [8192, 4096], P(('groups', 'ctx', 'head')), parts along dimension 0, may hold values from -6 to 6
- gain: float32 [4096], P('head'), may hold values from 0.5 to 1.5
Outputs:
- mixed: bfloat16 [8192, 4096], P(('groups', 'ctx', 'head')), parts along dimension 0
There are 2 independent parts, one for each index of `groups`. A program takes and returns all parts, laid end to end along the dimension named above; an argument that names none is the same for every part. Nothing has to cross between parts.
Inputs may be any that keep to these rules, and one draw needn't show every extreme that they name: `queries`: query entries lie in the stated range.
All inputs are finite; a program needn't handle non-finite values.
Results may differ from a plain program's by a relative error of at most 0.0054.
Values may be sent and summed in bfloat16 or wider, within the bound.
No kernel may reach another device: no remote copies, remote signals or barrier semaphores. Data moves between devices by JAX's collectives and lax.ppermute only.
A program may use at most 128 MiB of HBM per device.

v0:
```python
import math
import jax
import jax.numpy as jnp
from jax import lax
from jax.sharding import PartitionSpec as P

HEADS = 32
KD = 16
VD = 128
WINDOW = 64
outer_scale = 1.0 / (4.0 * math.sqrt(2.0))
epsilon = 1e-06


def shifted(shard, axis, by):
    peers = lax.axis_size(axis)
    pairs = [(i, i + by) for i in range(peers) if 0 <= i + by < peers]
    return lax.ppermute(shard, axis, pairs)


def entering(shard, axis, combine, identity):
    peers, here = (lax.axis_size(axis), lax.axis_index(axis))
    everything = lax.all_gather(shard, axis)
    start = jnp.broadcast_to(jnp.asarray(identity, shard.dtype), shard.shape)

    def hop(k, before):
        reached = k < here
        new = combine(before, everything[k])
        return jnp.where(reached, new, before)

    return lax.fori_loop(0, peers, hop, start)


def feature_map(vector):
    width = vector.shape[-1]
    products = (vector[..., :, None] * vector[..., None, :]).reshape(
        vector.shape[:-1] + (width * width,)
    )
    unit_column = jnp.ones(vector.shape[:-1] + (1,), jnp.float32)
    return jnp.concatenate([unit_column, vector * 0.5, products * outer_scale], axis=-1)


def per_device(queries, keys, values, gain):
    local_tokens = queries.shape[0]
    query_tok = queries.reshape(local_tokens, HEADS, KD)
    key_tok = keys.reshape(local_tokens, HEADS, KD)
    value_tok = values.reshape(local_tokens, HEADS, VD)
    query_head, key_head, value_head = (
        lax.all_to_all(query_tok, "head", split_axis=1, concat_axis=0, tiled=True),
        lax.all_to_all(key_tok, "head", split_axis=1, concat_axis=0, tiled=True),
        lax.all_to_all(value_tok, "head", split_axis=1, concat_axis=0, tiled=True),
    )
    span_rows = query_head.shape[0]
    heads_here = query_head.shape[1]
    block_rows = min(512, span_rows)
    block_count = span_rows // block_rows
    tail_keys, tail_values = shifted(
        (key_head[span_rows - WINDOW :], value_head[span_rows - WINDOW :]), "ctx", 1
    )
    key_ext = jnp.concatenate([tail_keys, key_head], axis=0)
    value_ext = jnp.concatenate([tail_values, value_head], axis=0)
    first_span = lax.axis_index("ctx") == 0
    key_features = feature_map(key_head.astype(jnp.float32)).astype(jnp.bfloat16)
    own_state = jnp.einsum(
        "bhf,bhv->hfv", key_features, value_head, preferred_element_type=jnp.float32
    )

    def combine_states(earlier, later):
        return earlier + later

    prefix = entering(own_state, "ctx", combine_states, jnp.zeros_like(own_state))

    def block_step(state, block_index):
        start = block_index * block_rows
        query_block = lax.dynamic_slice_in_dim(query_head, start, block_rows, 0)
        key_block = lax.dynamic_slice_in_dim(key_head, start, block_rows, 0)
        value_block = lax.dynamic_slice_in_dim(value_head, start, block_rows, 0)
        key_feat = lax.dynamic_slice_in_dim(key_features, start, block_rows, 0)
        key_window = lax.dynamic_slice_in_dim(key_ext, start, block_rows + WINDOW, 0)
        value_window = lax.dynamic_slice_in_dim(value_ext, start, block_rows + WINDOW, 0)
        scores = (
            jnp.einsum("bhd,chd->hbc", query_block, key_block, preferred_element_type=jnp.float32)
            * 0.25
        )
        row_pos = jnp.arange(block_rows)[:, None]
        col_pos = jnp.arange(block_rows)[None, :]
        kernel = jnp.where(col_pos <= row_pos, 1.0 + scores + 0.5 * scores * scores, 0.0).astype(
            jnp.bfloat16
        )
        intra = jnp.einsum("hbc,chv->bhv", kernel, value_block, preferred_element_type=jnp.float32)
        query_feat = feature_map(query_block.astype(jnp.float32)).astype(jnp.bfloat16)
        inter = jnp.einsum(
            "bhf,hfv->bhv",
            query_feat,
            state.astype(jnp.bfloat16),
            preferred_element_type=jnp.float32,
        )
        state = state + jnp.einsum(
            "bhf,bhv->hfv", key_feat, value_block, preferred_element_type=jnp.float32
        )
        window_scores = (
            jnp.einsum("bhd,chd->hbc", query_block, key_window, preferred_element_type=jnp.float32)
            * 0.25
        )
        key_pos = jnp.arange(block_rows + WINDOW)[None, :] - WINDOW
        valid = (
            (key_pos <= row_pos)
            & (key_pos > row_pos - WINDOW)
            & ((start + key_pos >= 0) | jnp.logical_not(first_span))
        )
        masked = jnp.where(valid, window_scores, -jnp.inf)
        highest_score = jnp.max(masked, axis=2, keepdims=True)
        expo = jnp.where(valid, jnp.exp(window_scores - highest_score), 0.0)
        weights = (expo / jnp.sum(expo, axis=2, keepdims=True)).astype(jnp.bfloat16)
        window_out = jnp.einsum(
            "hbc,chv->bhv", weights, value_window, preferred_element_type=jnp.float32
        )
        return (state, (intra + inter, window_out))

    final_state, (linear_all, window_all) = lax.scan(block_step, prefix, jnp.arange(block_count))
    linear = linear_all.reshape(span_rows, heads_here, VD)
    window = window_all.reshape(span_rows, heads_here, VD)
    scale = lax.rsqrt(jnp.mean(linear * linear, axis=2, keepdims=True) + epsilon)
    gains = gain.reshape(heads_here, VD)
    mixed = (linear * scale * gains + window).astype(jnp.bfloat16)
    tokens_back = lax.all_to_all(mixed, "head", split_axis=0, concat_axis=1, tiled=True)
    return tokens_back.reshape(tokens_back.shape[0], HEADS * VD)


def solution(mesh):
    placed = (
        P(("groups", "ctx", "head"), None),
        P(("groups", "ctx", "head"), None),
        P(("groups", "ctx", "head"), None),
        P("head"),
    )
    return jax.shard_map(
        per_device,
        mesh=mesh,
        in_specs=placed,
        out_specs=P(("groups", "ctx", "head"), None),
        check_vma=False,
    )
```

profile of v0, /device:TPU:0, one launch (start us, length us, event | category | flops | bytes accessed | tf_op | source)
XLA Modules:
  0.0 278.9 jit_solution(16457745592861958230)
XLA Ops:
  8.3 4.2 %all-to-all-start = ((bf16[256,32,16]{0,2,1:T(8,128)(2,1)}), bf16[256,32,16]{0,2,1:T(8,128)(2,1)S(1)}, u32[]{:S(2)}, u32[]{:S(2)}) async-start(bf16[256,32,16]{0,2,1:T(8,128)(2,1)} %bitcast.7), calls=%async_computation | async-start | bytes 524288 | tf_op jit(solution)/shard_map/all_to_all | solution.py:50
  18.7 3.6 %all-to-all-start.1 = ((bf16[256,32,128]{2,0,1:T(8,128)(2,1)}), bf16[256,32,128]{2,0,1:T(8,128)(2,1)S(1)}, u32[]{:S(2)}, u32[]{:S(2)}) async-start(bf16[256,32,128]{2,0,1:T(8,128)(2,1)} %copy.45), calls=%async_computation.1 | async-start | bytes 4194304 | tf_op jit(solution)/shard_map/all_to_all | solution.py:51
  23.8 3.9 %pad_maximum_fusion = bf16[1024,8,273]{0,2,1:T(8,128)(2,1)} fusion(bf16[1024,8,256]{0,2,1:T(8,128)(2,1)S(1)} %bitcast.76, bf16[1024,8,16]{0,2,1:T(8,128)(2,1)S(1)} %multiply_convert_fusion.3, bf16[273]{0:T(512)(128)(2,1)S(1)} %pad.7.clone), kind=kLoop, calls=%fused_computation.66 | loop fusion | flops 13418496 | bytes 8929826 | tf_op jit(solution)/shard_map/concatenate | solution.py:40
  27.7 20.3 %all-to-all-done.1 = bf16[256,32,128]{2,0,1:T(8,128)(2,1)S(1)} async-done(((bf16[256,32,128]{2,0,1:T(8,128)(2,1)}), bf16[256,32,128]{2,0,1:T(8,128)(2,1)S(1)}, u32[]{:S(2)}, u32[]{:S(2)}) %all-to-all-start.1) | async-done | bytes 2097184 | tf_op jit(solution)/shard_map/all_to_all | solution.py:51
  49.4 4.4 %fusion.77 = f32[8,273,128]{2,1,0:T(8,128)S(1)} fusion(bf16[1024,8,273]{0,2,1:T(8,128)(2,1)} %pad_maximum_fusion, bf16[1024,8,128]{2,0,1:T(8,128)(2,1)} %bitcast.15), kind=kOutput, calls=%fused_computation.77 | convolution fusion | flops 572522496 | bytes 7688192 | tf_op jit(solution)/shard_map/bhf,bhv->hfv/dot_general | solution.py:64
  55.9 3.4 %all-to-all-start.2 = ((bf16[256,32,16]{0,2,1:T(8,128)(2,1)}), bf16[256,32,16]{0,2,1:T(8,128)(2,1)S(1)}, u32[]{:S(2)}, u32[]{:S(2)}) async-start(bf16[256,32,16]{0,2,1:T(8,128)(2,1)} %bitcast.17), calls=%async_computation.2 | async-start | bytes 524288 | tf_op jit(solution)/shard_map/all_to_all | solution.py:49
  59.4 4.1 %collective-permute-start.1 = (bf16[64,8,16]{0,2,1:T(8,128)(2,1)S(1)}, bf16[64,8,16]{0,2,1:T(8,128)(2,1)S(1)}, u32[]{:S(2)}, u32[]{:S(2)}) collective-permute-start(bf16[64,8,16]{0,2,1:T(8,128)(2,1)S(1)} %slice.9), channel_id=1, source_target_pairs={{0,4},{4,8},{8,12},{1,5},{5,9},{9,13},{2,6},{6,10},{10,14},{3,7},{... | collective-permute-start | bytes 49160 | tf_op jit(solution)/shard_map/ppermute | solution.py:18
  67.0 4.3 %collective-permute-start = (bf16[64,8,128]{2,0,1:T(8,128)(2,1)S(1)}, bf16[64,8,128]{2,0,1:T(8,128)(2,1)S(1)}, u32[]{:S(2)}, u32[]{:S(2)}) collective-permute-start(bf16[64,8,128]{2,0,1:T(8,128)(2,1)S(1)} %slice.8), channel_id=1, source_target_pairs={{0,4},{4,8},{8,12},{1,5},{5,9},{9,13},{2,6},{6,10},{10,14},{3,7},{... | collective-permute-start | bytes 393224 | tf_op jit(solution)/shard_map/ppermute | solution.py:18
  72.2 5.1 %collective-permute-done = bf16[64,8,128]{2,0,1:T(8,128)(2,1)S(1)} collective-permute-done((bf16[64,8,128]{2,0,1:T(8,128)(2,1)S(1)}, bf16[64,8,128]{2,0,1:T(8,128)(2,1)S(1)}, u32[]{:S(2)}, u32[]{:S(2)}) %collective-permute-start) | collective-permute-done | bytes 131104 | tf_op jit(solution)/shard_map/ppermute | solution.py:18
  80.5 65.2 %all-gather.3.cloned.1.call-done = f32[32,273,128]{2,0,1:T(8,128)} async-done(((f32[8,273,128]{2,0,1:T(8,128)}), f32[32,273,128]{2,0,1:T(8,128)}) %all-gather.3.cloned.1.call-update) | async-done | bytes 4472848 | tf_op jit(solution)/shard_map/all_gather | solution.py:23
  145.7 7.5 %while.32 = (s32[]{:T(128)}, f32[8,273,128]{2,1,0:T(8,128)S(1)}, s32[]{:T(128)}, f32[4,8,273,128]{3,1,0,2:T(8,128)}, s32[]{:T(128)}, /*index=5*/s32[]{:T(128)}) while((s32[]{:T(128)}, f32[8,273,128]{2,1,0:T(8,128)S(1)}, s32[]{:T(128)}, f32[4,8,273,128]{3,1,0,2:T(8,128)}, s32[]{:T(128)}, /*index=5*/s32[]{:T(128)}) %tuple.69), condition=%wide.region_1.2_spmd.clone, body=%wide.region_0.1_spmd.clone.sunk | while | flops 838660 | bytes 5591141 | solution.py:31
  153.2 71.0 %while.31 = (s32[]{:T(128)}, f32[8,273,128]{2,1,0:T(8,128)S(1)}, f32[2,512,8,128]{1,3,2,0:T(8,128)}, f32[2,512,8,128]{3,2,1,0:T(8,128)}, s32[2]{0:T(128)S(1)}, /...) while((s32[]{:T(128)}, f32[8,273,128]{2,1,0:T(8,128)S(1)}, ...), condition=%wide.region_5.6_spmd, body=%wide.region_2.5_spmd.sunk | while | flops 1977677568 | bytes 70311560 | solution.py:120
  158.9 4.5 %fusion.111 = f32[8,128,512]{2,1,0:T(8,128)S(1)} fusion(pred[512,512]{1,0:T(8,128)(4,1)} %iota_compare_fusion.3, bf16[1024,8,128]{2,0,1:T(8,128)(2,1)} %get-tuple-element.495, s32[]{:T(128)S(6)} %select_n.84, bf16[1024,8,16]{0,2,1:T(8,128)(2,1)} %copy-done.1, bf16[1024,8,16]{0,2,1:T(8,128)(2,1)} %get-tuple-element.496), kind=kOutput, calls=%fused_computation.12.clone.1 | convolution fusion | flops 618659840 | bytes 3671552 | tf_op jit(solution)/shard_map/while/body/eval_jaxpr/hbc,chv->bhv/dot_general | solution.py:90
  164.2 3.7 %bitcast_dynamic-update-slice_fusion.2 = f32[2,512,8,128]{1,3,2,0:T(8,128)} fusion(f32[2,512,8,128]{1,3,2,0:T(8,128)} %get-tuple-element.472, s32[]{:T(128)S(6)} %copy.85, f32[8,128,512]{2,1,0:T(8,128)S(1)} %fusion.111, bf16[512,8,256]{0,2,1:T(8,128)(2,1)S(1)} %bitcast.73, bf16[512,8,16]{0,2,1:T(8,128)(2,1)} %multiply_convert_fusion.7, ...), kind=kOutput, calls=%fused_computation.22.clone.1 | convolution fusion | flops 293774336 | bytes 7541286 | tf_op jit(solution)/shard_map/while/body/eval_jaxpr/bhf,hfv->bhv/dot_general | solution.py:92
  170.2 8.4 %fusion.114 = (f32[8,512]{1,0:T(8,128)S(1)}, f32[8,512,576]{1,2,0:T(8,128)}) fusion(pred[512,576]{0,1:T(8,128)(4,1)S(1)} %copy-done, bf16[1088,8,16]{0,2,1:T(8,128)(2,1)S(1)} %copy-done.3, s32[]{:T(128)S(6)} %select_n.85, bf16[1024,8,16]{0,2,1:T(8,128)(2,1)} %get-tuple-element.496, s32[]{:T(128)S(6)} %select_n.84), kind=kOutput, calls=%fused_computation.76.clone.1 | convolution fusion | flops 165151296 | bytes 10635264 | tf_op jit(solution)/shard_map/while/body/eval_jaxpr/sub | solution.py:113
  178.6 6.5 %fusion.115 = f32[1,512,8,128]{1,3,2,0:T(8,128)} fusion(f32[8,512,576]{1,2,0:T(8,128)} %get-tuple-element.427, f32[8,512]{1,0:T(8,128)S(1)} %get-tuple-element.428, bf16[1088,8,128]{2,0,1:T(8,128)(2,1)} %get-tuple-element.498, s32[]{:T(128)S(6)} %select_n.85), kind=kOutput, calls=%fused_computation.24.clone.1 | convolution fusion | flops 608698368 | bytes 12730372 | tf_op jit(solution)/shard_map/while/body/eval_jaxpr/hbc,chv->bhv/dot_general | solution.py:115
  194.4 4.6 %fusion.111 = f32[8,128,512]{2,1,0:T(8,128)S(1)} fusion(pred[512,512]{1,0:T(8,128)(4,1)} %iota_compare_fusion.3, bf16[1024,8,128]{2,0,1:T(8,128)(2,1)} %get-tuple-element.495, s32[]{:T(128)S(6)} %select_n.84, bf16[1024,8,16]{0,2,1:T(8,128)(2,1)} %copy-done.1, bf16[1024,8,16]{0,2,1:T(8,128)(2,1)} %get-tuple-element.496), kind=kOutput, calls=%fused_computation.12.clone.1 | convolution fusion | flops 618659840 | bytes 3671552 | tf_op jit(solution)/shard_map/while/body/eval_jaxpr/hbc,chv->bhv/dot_general | solution.py:90
  199.6 3.7 %bitcast_dynamic-update-slice_fusion.2 = f32[2,512,8,128]{1,3,2,0:T(8,128)} fusion(f32[2,512,8,128]{1,3,2,0:T(8,128)} %get-tuple-element.472, s32[]{:T(128)S(6)} %copy.85, f32[8,128,512]{2,1,0:T(8,128)S(1)} %fusion.111, bf16[512,8,256]{0,2,1:T(8,128)(2,1)S(1)} %bitcast.73, bf16[512,8,16]{0,2,1:T(8,128)(2,1)} %multiply_convert_fusion.7, ...), kind=kOutput, calls=%fused_computation.22.clone.1 | convolution fusion | flops 293774336 | bytes 7541286 | tf_op jit(solution)/shard_map/while/body/eval_jaxpr/bhf,hfv->bhv/dot_general | solution.py:92
  205.7 8.4 %fusion.114 = (f32[8,512]{1,0:T(8,128)S(1)}, f32[8,512,576]{1,2,0:T(8,128)}) fusion(pred[512,576]{0,1:T(8,128)(4,1)S(1)} %copy-done, bf16[1088,8,16]{0,2,1:T(8,128)(2,1)S(1)} %copy-done.3, s32[]{:T(128)S(6)} %select_n.85, bf16[1024,8,16]{0,2,1:T(8,128)(2,1)} %get-tuple-element.496, s32[]{:T(128)S(6)} %select_n.84), kind=kOutput, calls=%fused_computation.76.clone.1 | convolution fusion | flops 165151296 | bytes 10635264 | tf_op jit(solution)/shard_map/while/body/eval_jaxpr/sub | solution.py:113
  214.1 6.5 %fusion.115 = f32[1,512,8,128]{1,3,2,0:T(8,128)} fusion(f32[8,512,576]{1,2,0:T(8,128)} %get-tuple-element.427, f32[8,512]{1,0:T(8,128)S(1)} %get-tuple-element.428, bf16[1088,8,128]{2,0,1:T(8,128)(2,1)} %get-tuple-element.498, s32[]{:T(128)S(6)} %select_n.85), kind=kOutput, calls=%fused_computation.24.clone.1 | convolution fusion | flops 608698368 | bytes 12730372 | tf_op jit(solution)/shard_map/while/body/eval_jaxpr/hbc,chv->bhv/dot_general | solution.py:115
  227.0 5.3 %copy.52 = f32[2,512,8,128]{3,2,1,0:T(8,128)} copy(f32[2,512,8,128]{1,3,2,0:T(8,128)} %get-tuple-element.272) | data formatting | bytes 8388608 | tf_op jit(solution)/shard_map/while | solution.py:120
  232.5 4.1 %fusion.66 = bf16[1024,8,128]{2,1,0:T(8,128)(2,1)S(1)} fusion(f32[2,512,8,128]{3,2,1,0:T(8,128)} %get-tuple-element.273, f32[2,512,8,128]{3,2,1,0:T(8,128)} %copy.52, f32[8,128]{1,0:T(8,128)S(1)} %bitcast.90, f32[1024,8]{1,0:T(8,128)S(1)} %copy.53), kind=kLoop, calls=%fused_computation.68 | loop fusion | flops 4194304 | bytes 10522624 | tf_op jit(solution)/shard_map/convert_element_type | solution.py:125
  236.6 28.8 %all_to_all.69 = bf16[1024,8,128]{2,1,0:T(8,128)(2,1)S(1)} all-to-all(bf16[1024,8,128]{2,1,0:T(8,128)(2,1)S(1)} %fusion.66), channel_id=1, replica_groups=mesh['groups'=2,'ctx'=4,'head'=4] {'head'}, dimensions={0} | all-to-all | bytes 4194304 | tf_op jit(solution)/shard_map/all_to_all | solution.py:126
  268.0 4.1 %copy.56 = bf16[256,4096]{1,0:T(8,128)(2,1)} copy(bf16[256,4096]{0,1:T(8,128)(2,1)} %bitcast.79) | data formatting | bytes 4194304 | tf_op jit(solution)/shard_map/reshape | solution.py:127
  (93 shorter events, 56.7 us)
Async XLA Ops:
  8.3 10.3 %all-to-all-start = ((bf16[256,32,16]{0,2,1:T(8,128)(2,1)}), bf16[256,32,16]{0,2,1:T(8,128)(2,1)S(1)}, u32[]{:S(2)}, u32[]{:S(2)}) async-start(bf16[256,32,16]{0,2,1:T(8,128)(2,1)} %bitcast.7), calls=%async_computation | async-start | bytes 524288 | tf_op jit(solution)/shard_map/all_to_all | solution.py:50
  18.7 29.3 %all-to-all-start.1 = ((bf16[256,32,128]{2,0,1:T(8,128)(2,1)}), bf16[256,32,128]{2,0,1:T(8,128)(2,1)S(1)}, u32[]{:S(2)}, u32[]{:S(2)}) async-start(bf16[256,32,128]{2,0,1:T(8,128)(2,1)} %copy.45), calls=%async_computation.1 | async-start | bytes 4194304 | tf_op jit(solution)/shard_map/all_to_all | solution.py:51
  22.3 123.4 %all-gather.3.cloned.1.call-start = ((), (), s32[]{:S(2)}) async-start(), calls=%async_computation.4 | async-start | bytes 5591040 | tf_op jit(solution)/shard_map/all_gather | solution.py:23
  49.4 5.7 %copy-start.4 = (bf16[256,512]{1,0:T(8,128)(2,1)S(1)}, bf16[256,512]{1,0:T(8,128)(2,1)}, u32[]{:S(2)}) copy-start(bf16[256,512]{1,0:T(8,128)(2,1)} %param.8) | copy-start | bytes 786436
  55.9 9.4 %all-to-all-start.2 = ((bf16[256,32,16]{0,2,1:T(8,128)(2,1)}), bf16[256,32,16]{0,2,1:T(8,128)(2,1)S(1)}, u32[]{:S(2)}, u32[]{:S(2)}) async-start(bf16[256,32,16]{0,2,1:T(8,128)(2,1)} %bitcast.17), calls=%async_computation.2 | async-start | bytes 524288 | tf_op jit(solution)/shard_map/all_to_all | solution.py:49
  59.4 11.9 %collective-permute-start.1 = (bf16[64,8,16]{0,2,1:T(8,128)(2,1)S(1)}, bf16[64,8,16]{0,2,1:T(8,128)(2,1)S(1)}, u32[]{:S(2)}, u32[]{:S(2)}) collective-permute-start(bf16[64,8,16]{0,2,1:T(8,128)(2,1)S(1)} %slice.9), channel_id=1, source_target_pairs={{0,4},{4,8},{8,12},{1,5},{5,9},{9,13},{2,6},{6,10},{10,14},{3,7},{... | collective-permute-start | bytes 49160 | tf_op jit(solution)/shard_map/ppermute | solution.py:18
  67.0 10.3 %collective-permute-start = (bf16[64,8,128]{2,0,1:T(8,128)(2,1)S(1)}, bf16[64,8,128]{2,0,1:T(8,128)(2,1)S(1)}, u32[]{:S(2)}, u32[]{:S(2)}) collective-permute-start(bf16[64,8,128]{2,0,1:T(8,128)(2,1)S(1)} %slice.8), channel_id=1, source_target_pairs={{0,4},{4,8},{8,12},{1,5},{5,9},{9,13},{2,6},{6,10},{10,14},{3,7},{... | collective-permute-start | bytes 393224 | tf_op jit(solution)/shard_map/ppermute | solution.py:18
  153.2 4.6 %copy-start.1 = (bf16[1024,8,16]{0,2,1:T(8,128)(2,1)}, bf16[1024,8,16]{0,2,1:T(8,128)(2,1)S(1)}, u32[]{:S(2)}) copy-start(bf16[1024,8,16]{0,2,1:T(8,128)(2,1)S(1)} %get-tuple-element.497) | copy-start | bytes 786436 | tf_op jit(solution)/shard_map/while
  163.5 4.4 %slice-start = ((s8[4587520]{0:T(1024)(128)(4,1)}), s8[4194304]{0:T(1024)(128)(4,1)S(1)}, s32[]{:S(2)}) async-start(s8[4587520]{0:T(1024)(128)(4,1)} %bitcast.74), calls=%async_computation.5 | async-start | bytes 8388608 | tf_op jit(solution)/shard_map/while
  164.2 3.7 %slice-start.1 = ((s8[4587520]{0:T(1024)(128)(4,1)}), s8[393216]{0:T(1024)(128)(4,1)S(1)}, s32[]{:S(2)}) async-start(s8[4587520]{0:T(1024)(128)(4,1)} %bitcast.74), calls=%async_computation.6 | async-start | bytes 786432 | tf_op jit(solution)/shard_map/while
  167.9 2.3 copy-start
  167.9 2.3 copy-start.3
  185.1 3.6 %copy-start.2 = (bf16[1024,8,16]{0,2,1:T(8,128)(2,1)S(1)}, bf16[1024,8,16]{0,2,1:T(8,128)(2,1)}, u32[]{:S(2)}) copy-start(bf16[1024,8,16]{0,2,1:T(8,128)(2,1)} %copy-done.1) | copy-start | bytes 786436 | tf_op jit(solution)/shard_map/while
  188.7 4.6 %copy-start.1 = (bf16[1024,8,16]{0,2,1:T(8,128)(2,1)}, bf16[1024,8,16]{0,2,1:T(8,128)(2,1)S(1)}, u32[]{:S(2)}) copy-start(bf16[1024,8,16]{0,2,1:T(8,128)(2,1)S(1)} %get-tuple-element.497) | copy-start | bytes 786436 | tf_op jit(solution)/shard_map/while
  198.9 4.4 %slice-start = ((s8[4587520]{0:T(1024)(128)(4,1)}), s8[4194304]{0:T(1024)(128)(4,1)S(1)}, s32[]{:S(2)}) async-start(s8[4587520]{0:T(1024)(128)(4,1)} %bitcast.74), calls=%async_computation.5 | async-start | bytes 8388608 | tf_op jit(solution)/shard_map/while
  199.6 3.7 %slice-start.1 = ((s8[4587520]{0:T(1024)(128)(4,1)}), s8[393216]{0:T(1024)(128)(4,1)S(1)}, s32[]{:S(2)}) async-start(s8[4587520]{0:T(1024)(128)(4,1)} %bitcast.74), calls=%async_computation.6 | async-start | bytes 786432 | tf_op jit(solution)/shard_map/while
  203.4 2.4 copy-start
  203.4 2.4 copy-start.3
  220.6 3.6 %copy-start.2 = (bf16[1024,8,16]{0,2,1:T(8,128)(2,1)S(1)}, bf16[1024,8,16]{0,2,1:T(8,128)(2,1)}, u32[]{:S(2)}) copy-start(bf16[1024,8,16]{0,2,1:T(8,128)(2,1)} %copy-done.1) | copy-start | bytes 786436 | tf_op jit(solution)/shard_map/while
  227.0 5.5 %copy-start.5 = (f32[1024]{0:T(1024)S(1)}, f32[1024]{0:T(1024)}, u32[]{:S(2)}) copy-start(f32[1024]{0:T(1024)} %param.11) | copy-start | bytes 12292
Sparse Core Ops, SparseCore 0:
  55.2 90.4 all-gather.2
where the time goes:
time: 280 us; the launch traced here: 279 us
  waiting for transfers between devices  92.4 us (33%)
  matrix products  55.3 us (20%)
  local copies, waits for them, and re-layouts  39.3 us (14%)
  blocking collectives  28.8 us (10%)
  other arithmetic  28.4 us (10%)
  starting transfers between devices  19.7 us (7%)
  between operations  13.6 us (5%)
    all_gather x1, waiting for transfers between devices, entering(): everything = lax.all_gather(shard, axis)  65.2 us
    all_to_all x1, blocking collectives, per_device(): lax.all_to_all(mixed, 'head', split_axis=0, concat_axis=1, tiled=True)  28.8 us
    all_to_all x1, waiting for transfers between devices, per_device(): lax.all_to_all(value_tok, 'head', split_axis=1, concat_axis=0, tiled=True)  20.3 us
    sub x2, matrix products, block_step(): expo = jnp.where(valid, jnp.exp(window_scores - highest_score), 0.0)  16.7 us
    dot_general x2, matrix products, block_step(): jnp.einsum('hbc,chv->bhv', weights, value_window, preferred_element_type=...  13 us
    dot_general x2, matrix products, block_step(): jnp.einsum('hbc,chv->bhv', kernel, value_block, preferred_element_type=jn...  9.1 us
    ppermute x2, starting transfers between devices, shifted(): return lax.ppermute(shard, axis, pairs)  8.46 us
    dot_general x2, matrix products, block_step(): jnp.einsum('bhf,hfv->bhv', query_feat, state.astype(jnp.bfloat16), prefer...  7.45 us
  transfers between devices with their start and end apart: 6, of which 4 were waited for; matrix products, arithmetic and copies ran while one was open for 6% of the time, Pallas kernels for 0%

commit v1 on v0

--- a/solution.py
+++ b/solution.py
@@ -46,7 +46,12 @@
     key_tok = keys.reshape(local_tokens, HEADS, KD)
     value_tok = values.reshape(local_tokens, HEADS, VD)
     query_head, key_head, value_head = (
-        lax.all_to_all(query_tok, "head", split_axis=1, concat_axis=0, tiled=True),
+        jnp.concatenate(
+            lax.all_to_all(
+                jnp.stack(jnp.split(query_tok, lax.axis_size("head"), axis=1)), "head", 0, 0
+            ),
+            axis=0,
+        ),
         lax.all_to_all(key_tok, "head", split_axis=1, concat_axis=0, tiled=True),
         lax.all_to_all(value_tok, "head", split_axis=1, concat_axis=0, tiled=True),
     )

time: 280 us -> 280 us (level)
  waiting for transfers between devices: 92.4 us -> 88.7 us
  other arithmetic: 28.4 us -> 32 us
    another operation x8 -> x9, other arithmetic: 5.83 us -> 7.56 us
  transfers between devices with their start and end apart: 6 -> 6, of which waited for: 4 -> 4; matrix products, arithmetic and copies ran while one was open for 6% -> 8% of each run, Pallas kernels for 0% -> 0%
where the time goes in v1:
time: 280 us; the launch traced here: 279 us
  waiting for transfers between devices  88.7 us (32%)
  matrix products  55.3 us (20%)
  local copies, waits for them, and re-layouts  39.8 us (14%)
  other arithmetic  32 us (11%)
  blocking collectives  28.4 us (10%)
  starting transfers between devices  19.7 us (7%)
  between operations  13.6 us (5%)
    all_gather x1, waiting for transfers between devices, entering(): everything = lax.all_gather(shard, axis)  65.9 us
    all_to_all x1, blocking collectives, per_device(): lax.all_to_all(mixed, 'head', split_axis=0, concat_axis=1, tiled=True)  28.4 us
    all_to_all x1, waiting for transfers between devices, per_device(): lax.all_to_all(value_tok, 'head', split_axis=1, concat_axis=0, tiled=True)  17.6 us
    sub x2, matrix products, block_step(): expo = jnp.where(valid, jnp.exp(window_scores - highest_score), 0.0)  16.7 us
    dot_general x2, matrix products, block_step(): jnp.einsum('hbc,chv->bhv', weights, value_window, preferred_element_type=...  13 us
    dot_general x2, matrix products, block_step(): jnp.einsum('hbc,chv->bhv', kernel, value_block, preferred_element_type=jn...  9.09 us
    ppermute x2, starting transfers between devices, shifted(): return lax.ppermute(shard, axis, pairs)  8.46 us
    dot_general x2, matrix products, block_step(): jnp.einsum('bhf,hfv->bhv', query_feat, state.astype(jnp.bfloat16), prefer...  7.46 us
  transfers between devices with their start and end apart: 6, of which 4 were waited for; matrix products, arithmetic and copies ran while one was open for 8% of the time, Pallas kernels for 0%

profile of v1, /device:TPU:0, one launch (start us, length us, event | category | flops | bytes accessed | tf_op | source)
XLA Modules:
  0.0 279.0 jit_solution(16212991702656598304)
XLA Ops:
  8.3 4.2 %all-to-all-start = ((bf16[256,32,16]{0,2,1:T(8,128)(2,1)}), bf16[256,32,16]{0,2,1:T(8,128)(2,1)S(1)}, u32[]{:S(2)}, u32[]{:S(2)}) async-start(bf16[256,32,16]{0,2,1:T(8,128)(2,1)} %bitcast.7), calls=%async_computation | async-start | bytes 524288 | tf_op jit(solution)/shard_map/all_to_all | solution.py:55
  18.7 3.6 %all-to-all-start.1 = ((bf16[256,32,128]{2,0,1:T(8,128)(2,1)}), bf16[256,32,128]{2,0,1:T(8,128)(2,1)S(1)}, u32[]{:S(2)}, u32[]{:S(2)}) async-start(bf16[256,32,128]{2,0,1:T(8,128)(2,1)} %copy.49), calls=%async_computation.1 | async-start | bytes 4194304 | tf_op jit(solution)/shard_map/all_to_all | solution.py:56
  26.5 3.9 %pad_maximum_fusion = bf16[1024,8,273]{0,2,1:T(8,128)(2,1)} fusion(bf16[1024,8,256]{0,2,1:T(8,128)(2,1)S(1)} %bitcast.81, bf16[1024,8,16]{0,2,1:T(8,128)(2,1)S(1)} %multiply_convert_fusion.3, bf16[273]{0:T(512)(128)(2,1)S(1)} %pad.11.clone), kind=kLoop, calls=%fused_computation.66 | loop fusion | flops 13418496 | bytes 8929826 | tf_op jit(solution)/shard_map/concatenate | solution.py:40
  30.4 17.6 %all-to-all-done.1 = bf16[256,32,128]{2,0,1:T(8,128)(2,1)S(1)} async-done(((bf16[256,32,128]{2,0,1:T(8,128)(2,1)}), bf16[256,32,128]{2,0,1:T(8,128)(2,1)S(1)}, u32[]{:S(2)}, u32[]{:S(2)}) %all-to-all-start.1) | async-done | bytes 2097184 | tf_op jit(solution)/shard_map/all_to_all | solution.py:56
  49.4 4.4 %fusion.77 = f32[8,273,128]{2,1,0:T(8,128)S(1)} fusion(bf16[1024,8,273]{0,2,1:T(8,128)(2,1)} %pad_maximum_fusion, bf16[1024,8,128]{2,0,1:T(8,128)(2,1)} %bitcast.15), kind=kOutput, calls=%fused_computation.82 | convolution fusion | flops 572522496 | bytes 7688192 | tf_op jit(solution)/shard_map/bhf,bhv->hfv/dot_general | solution.py:69
  56.0 3.4 %all-to-all-start.2 = ((bf16[4,256,8,16]{1,3,2,0:T(8,128)(2,1)}), bf16[4,256,8,16]{1,3,2,0:T(8,128)(2,1)S(1)}, u32[]{:S(2)}, u32[]{:S(2)}) async-start(bf16[4,256,8,16]{1,3,2,0:T(8,128)(2,1)} %pad_maximum_fusion.3), calls=%async_computation.2 | async-start | bytes 524288 | tf_op jit(solution)/shard_map/all_to_all | solution.py:50
  60.3 4.1 %collective-permute-start.1 = (bf16[64,8,16]{0,2,1:T(8,128)(2,1)S(1)}, bf16[64,8,16]{0,2,1:T(8,128)(2,1)S(1)}, u32[]{:S(2)}, u32[]{:S(2)}) collective-permute-start(bf16[64,8,16]{0,2,1:T(8,128)(2,1)S(1)} %slice.9), channel_id=1, source_target_pairs={{0,4},{4,8},{8,12},{1,5},{5,9},{9,13},{2,6},{6,10},{10,14},{3,7},{... | collective-permute-start | bytes 49160 | tf_op jit(solution)/shard_map/ppermute | solution.py:18
  67.1 4.3 %collective-permute-start = (bf16[64,8,128]{2,0,1:T(8,128)(2,1)S(1)}, bf16[64,8,128]{2,0,1:T(8,128)(2,1)S(1)}, u32[]{:S(2)}, u32[]{:S(2)}) collective-permute-start(bf16[64,8,128]{2,0,1:T(8,128)(2,1)S(1)} %slice.8), channel_id=1, source_target_pairs={{0,4},{4,8},{8,12},{1,5},{5,9},{9,13},{2,6},{6,10},{10,14},{3,7},{... | collective-permute-start | bytes 393224 | tf_op jit(solution)/shard_map/ppermute | solution.py:18
  73.3 4.2 %collective-permute-done = bf16[64,8,128]{2,0,1:T(8,128)(2,1)S(1)} collective-permute-done((bf16[64,8,128]{2,0,1:T(8,128)(2,1)S(1)}, bf16[64,8,128]{2,0,1:T(8,128)(2,1)S(1)}, u32[]{:S(2)}, u32[]{:S(2)}) %collective-permute-start) | collective-permute-done | bytes 131104 | tf_op jit(solution)/shard_map/ppermute | solution.py:18
  80.6 65.9 %all-gather.3.cloned.1.call-done = f32[32,273,128]{2,0,1:T(8,128)} async-done(((f32[8,273,128]{2,0,1:T(8,128)}), f32[32,273,128]{2,0,1:T(8,128)}) %all-gather.3.cloned.1.call-update) | async-done | bytes 4472848 | tf_op jit(solution)/shard_map/all_gather | solution.py:23
  146.4 7.5 %while.32 = (s32[]{:T(128)}, f32[8,273,128]{2,1,0:T(8,128)S(1)}, s32[]{:T(128)}, f32[4,8,273,128]{3,1,0,2:T(8,128)}, s32[]{:T(128)}, /*index=5*/s32[]{:T(128)}) while((s32[]{:T(128)}, f32[8,273,128]{2,1,0:T(8,128)S(1)}, s32[]{:T(128)}, f32[4,8,273,128]{3,1,0,2:T(8,128)}, s32[]{:T(128)}, /*index=5*/s32[]{:T(128)}) %tuple.72), condition=%wide.region_1.2_spmd.clone, body=%wide.region_0.1_spmd.clone.sunk | while | flops 838660 | bytes 5591141 | solution.py:31
  154.0 70.8 %while.31 = (s32[]{:T(128)}, f32[8,273,128]{2,1,0:T(8,128)S(1)}, f32[2,512,8,128]{1,3,2,0:T(8,128)}, f32[2,512,8,128]{3,2,1,0:T(8,128)}, s32[2]{0:T(128)S(1)}, /...) while((s32[]{:T(128)}, f32[8,273,128]{2,1,0:T(8,128)S(1)}, ...), condition=%wide.region_5.6_spmd, body=%wide.region_2.5_spmd.sunk | while | flops 1977677568 | bytes 68214352 | solution.py:125
  159.6 4.5 %fusion.111 = f32[8,128,512]{2,1,0:T(8,128)S(1)} fusion(pred[512,512]{1,0:T(8,128)(4,1)} %iota_compare_fusion.3, bf16[1024,8,128]{2,0,1:T(8,128)(2,1)} %get-tuple-element.499, s32[]{:T(128)S(6)} %select_n.84, bf16[1024,8,16]{0,2,1:T(8,128)(2,1)} %get-tuple-element.501, bf16[1024,8,16]{0,2,1:T(8,128)(2,1)} %get-tuple-element.500), kind=kOutput, calls=%fused_computation.12.clone.1 | convolution fusion | flops 618659840 | bytes 3671552 | tf_op jit(solution)/shard_map/while/body/eval_jaxpr/hbc,chv->bhv/dot_general | solution.py:95
  164.9 3.7 %bitcast_dynamic-update-slice_fusion.2 = f32[2,512,8,128]{1,3,2,0:T(8,128)} fusion(f32[2,512,8,128]{1,3,2,0:T(8,128)} %get-tuple-element.476, s32[]{:T(128)S(6)} %copy.89, f32[8,128,512]{2,1,0:T(8,128)S(1)} %fusion.111, bf16[512,8,256]{0,2,1:T(8,128)(2,1)S(1)} %bitcast.78, bf16[512,8,16]{0,2,1:T(8,128)(2,1)} %multiply_convert_fusion.7, ...), kind=kOutput, calls=%fused_computation.22.clone.1 | convolution fusion | flops 293774336 | bytes 7541286 | tf_op jit(solution)/shard_map/while/body/eval_jaxpr/bhf,hfv->bhv/dot_general | solution.py:97
  170.9 8.3 %fusion.114 = (f32[8,512]{1,0:T(8,128)S(1)}, f32[8,512,576]{1,2,0:T(8,128)}) fusion(pred[512,576]{0,1:T(8,128)(4,1)S(1)} %copy-done, bf16[1088,8,16]{0,2,1:T(8,128)(2,1)S(1)} %copy-done.1, s32[]{:T(128)S(6)} %select_n.85, bf16[1024,8,16]{0,2,1:T(8,128)(2,1)} %get-tuple-element.500, s32[]{:T(128)S(6)} %select_n.84), kind=kOutput, calls=%fused_computation.81.clone.1 | convolution fusion | flops 165151296 | bytes 10635264 | tf_op jit(solution)/shard_map/while/body/eval_jaxpr/sub | solution.py:118
  179.3 6.5 %fusion.115 = f32[1,512,8,128]{1,3,2,0:T(8,128)} fusion(f32[8,512,576]{1,2,0:T(8,128)} %get-tuple-element.431, f32[8,512]{1,0:T(8,128)S(1)} %get-tuple-element.432, bf16[1088,8,128]{2,0,1:T(8,128)(2,1)} %get-tuple-element.502, s32[]{:T(128)S(6)} %select_n.85), kind=kOutput, calls=%fused_computation.24.clone.1 | convolution fusion | flops 608698368 | bytes 12730372 | tf_op jit(solution)/shard_map/while/body/eval_jaxpr/hbc,chv->bhv/dot_general | solution.py:120
  195.0 4.5 %fusion.111 = f32[8,128,512]{2,1,0:T(8,128)S(1)} fusion(pred[512,512]{1,0:T(8,128)(4,1)} %iota_compare_fusion.3, bf16[1024,8,128]{2,0,1:T(8,128)(2,1)} %get-tuple-element.499, s32[]{:T(128)S(6)} %select_n.84, bf16[1024,8,16]{0,2,1:T(8,128)(2,1)} %get-tuple-element.501, bf16[1024,8,16]{0,2,1:T(8,128)(2,1)} %get-tuple-element.500), kind=kOutput, calls=%fused_computation.12.clone.1 | convolution fusion | flops 618659840 | bytes 3671552 | tf_op jit(solution)/shard_map/while/body/eval_jaxpr/hbc,chv->bhv/dot_general | solution.py:95
  200.2 3.7 %bitcast_dynamic-update-slice_fusion.2 = f32[2,512,8,128]{1,3,2,0:T(8,128)} fusion(f32[2,512,8,128]{1,3,2,0:T(8,128)} %get-tuple-element.476, s32[]{:T(128)S(6)} %copy.89, f32[8,128,512]{2,1,0:T(8,128)S(1)} %fusion.111, bf16[512,8,256]{0,2,1:T(8,128)(2,1)S(1)} %bitcast.78, bf16[512,8,16]{0,2,1:T(8,128)(2,1)} %multiply_convert_fusion.7, ...), kind=kOutput, calls=%fused_computation.22.clone.1 | convolution fusion | flops 293774336 | bytes 7541286 | tf_op jit(solution)/shard_map/while/body/eval_jaxpr/bhf,hfv->bhv/dot_general | solution.py:97
  206.3 8.3 %fusion.114 = (f32[8,512]{1,0:T(8,128)S(1)}, f32[8,512,576]{1,2,0:T(8,128)}) fusion(pred[512,576]{0,1:T(8,128)(4,1)S(1)} %copy-done, bf16[1088,8,16]{0,2,1:T(8,128)(2,1)S(1)} %copy-done.1, s32[]{:T(128)S(6)} %select_n.85, bf16[1024,8,16]{0,2,1:T(8,128)(2,1)} %get-tuple-element.500, s32[]{:T(128)S(6)} %select_n.84), kind=kOutput, calls=%fused_computation.81.clone.1 | convolution fusion | flops 165151296 | bytes 10635264 | tf_op jit(solution)/shard_map/while/body/eval_jaxpr/sub | solution.py:118
  214.7 6.5 %fusion.115 = f32[1,512,8,128]{1,3,2,0:T(8,128)} fusion(f32[8,512,576]{1,2,0:T(8,128)} %get-tuple-element.431, f32[8,512]{1,0:T(8,128)S(1)} %get-tuple-element.432, bf16[1088,8,128]{2,0,1:T(8,128)(2,1)} %get-tuple-element.502, s32[]{:T(128)S(6)} %select_n.85), kind=kOutput, calls=%fused_computation.24.clone.1 | convolution fusion | flops 608698368 | bytes 12730372 | tf_op jit(solution)/shard_map/while/body/eval_jaxpr/hbc,chv->bhv/dot_general | solution.py:120
  227.5 5.3 %copy.56 = f32[2,512,8,128]{3,2,1,0:T(8,128)} copy(f32[2,512,8,128]{1,3,2,0:T(8,128)} %get-tuple-element.272) | data formatting | bytes 8388608 | tf_op jit(solution)/shard_map/while | solution.py:125
  233.0 4.1 %fusion.66 = bf16[1024,8,128]{2,1,0:T(8,128)(2,1)S(1)} fusion(f32[2,512,8,128]{3,2,1,0:T(8,128)} %get-tuple-element.273, f32[2,512,8,128]{3,2,1,0:T(8,128)} %copy.56, f32[8,128]{1,0:T(8,128)S(1)} %bitcast.91, f32[1024,8]{1,0:T(8,128)S(1)} %copy.57), kind=kLoop, calls=%fused_computation.68 | loop fusion | flops 4194304 | bytes 10522624 | tf_op jit(solution)/shard_map/convert_element_type | solution.py:130
  237.1 28.4 %all_to_all.56 = bf16[1024,8,128]{2,1,0:T(8,128)(2,1)S(1)} all-to-all(bf16[1024,8,128]{2,1,0:T(8,128)(2,1)S(1)} %fusion.66), channel_id=1, replica_groups=mesh['groups'=2,'ctx'=4,'head'=4] {'head'}, dimensions={0} | all-to-all | bytes 4194304 | tf_op jit(solution)/shard_map/all_to_all | solution.py:131
  268.1 4.1 %copy.60 = bf16[256,4096]{1,0:T(8,128)(2,1)} copy(bf16[256,4096]{0,1:T(8,128)(2,1)} %bitcast.84) | data formatting | bytes 4194304 | tf_op jit(solution)/shard_map/reshape | solution.py:132
  (87 shorter events, 60.2 us)
Async XLA Ops:
  8.3 10.3 %all-to-all-start = ((bf16[256,32,16]{0,2,1:T(8,128)(2,1)}), bf16[256,32,16]{0,2,1:T(8,128)(2,1)S(1)}, u32[]{:S(2)}, u32[]{:S(2)}) async-start(bf16[256,32,16]{0,2,1:T(8,128)(2,1)} %bitcast.7), calls=%async_computation | async-start | bytes 524288 | tf_op jit(solution)/shard_map/all_to_all | solution.py:55
  18.7 29.3 %all-to-all-start.1 = ((bf16[256,32,128]{2,0,1:T(8,128)(2,1)}), bf16[256,32,128]{2,0,1:T(8,128)(2,1)S(1)}, u32[]{:S(2)}, u32[]{:S(2)}) async-start(bf16[256,32,128]{2,0,1:T(8,128)(2,1)} %copy.49), calls=%async_computation.1 | async-start | bytes 4194304 | tf_op jit(solution)/shard_map/all_to_all | solution.py:56
  22.3 124.1 %all-gather.3.cloned.1.call-start = ((), (), s32[]{:S(2)}) async-start(), calls=%async_computation.4 | async-start | bytes 5591040 | tf_op jit(solution)/shard_map/all_gather | solution.py:23
  49.4 5.7 %copy-start.2 = (bf16[256,512]{1,0:T(8,128)(2,1)S(1)}, bf16[256,512]{1,0:T(8,128)(2,1)}, u32[]{:S(2)}) copy-start(bf16[256,512]{1,0:T(8,128)(2,1)} %param.8) | copy-start | bytes 786436
  56.0 9.4 %all-to-all-start.2 = ((bf16[4,256,8,16]{1,3,2,0:T(8,128)(2,1)}), bf16[4,256,8,16]{1,3,2,0:T(8,128)(2,1)S(1)}, u32[]{:S(2)}, u32[]{:S(2)}) async-start(bf16[4,256,8,16]{1,3,2,0:T(8,128)(2,1)} %pad_maximum_fusion.3), calls=%async_computation.2 | async-start | bytes 524288 | tf_op jit(solution)/shard_map/all_to_all | solution.py:50
  60.3 11.2 %collective-permute-start.1 = (bf16[64,8,16]{0,2,1:T(8,128)(2,1)S(1)}, bf16[64,8,16]{0,2,1:T(8,128)(2,1)S(1)}, u32[]{:S(2)}, u32[]{:S(2)}) collective-permute-start(bf16[64,8,16]{0,2,1:T(8,128)(2,1)S(1)} %slice.9), channel_id=1, source_target_pairs={{0,4},{4,8},{8,12},{1,5},{5,9},{9,13},{2,6},{6,10},{10,14},{3,7},{... | collective-permute-start | bytes 49160 | tf_op jit(solution)/shard_map/ppermute | solution.py:18
  67.1 10.3 %collective-permute-start = (bf16[64,8,128]{2,0,1:T(8,128)(2,1)S(1)}, bf16[64,8,128]{2,0,1:T(8,128)(2,1)S(1)}, u32[]{:S(2)}, u32[]{:S(2)}) collective-permute-start(bf16[64,8,128]{2,0,1:T(8,128)(2,1)S(1)} %slice.8), channel_id=1, source_target_pairs={{0,4},{4,8},{8,12},{1,5},{5,9},{9,13},{2,6},{6,10},{10,14},{3,7},{... | collective-permute-start | bytes 393224 | tf_op jit(solution)/shard_map/ppermute | solution.py:18
  164.2 4.4 %slice-start = ((s8[4587520]{0:T(1024)(128)(4,1)}), s8[4194304]{0:T(1024)(128)(4,1)S(1)}, s32[]{:S(2)}) async-start(s8[4587520]{0:T(1024)(128)(4,1)} %bitcast.79), calls=%async_computation.5 | async-start | bytes 8388608 | tf_op jit(solution)/shard_map/while
  164.8 3.7 %slice-start.1 = ((s8[4587520]{0:T(1024)(128)(4,1)}), s8[393216]{0:T(1024)(128)(4,1)S(1)}, s32[]{:S(2)}) async-start(s8[4587520]{0:T(1024)(128)(4,1)} %bitcast.79), calls=%async_computation.6 | async-start | bytes 786432 | tf_op jit(solution)/shard_map/while
  168.6 2.3 copy-start
  168.6 2.3 copy-start.1
  199.5 4.4 %slice-start = ((s8[4587520]{0:T(1024)(128)(4,1)}), s8[4194304]{0:T(1024)(128)(4,1)S(1)}, s32[]{:S(2)}) async-start(s8[4587520]{0:T(1024)(128)(4,1)} %bitcast.79), calls=%async_computation.5 | async-start | bytes 8388608 | tf_op jit(solution)/shard_map/while
  200.2 3.7 %slice-start.1 = ((s8[4587520]{0:T(1024)(128)(4,1)}), s8[393216]{0:T(1024)(128)(4,1)S(1)}, s32[]{:S(2)}) async-start(s8[4587520]{0:T(1024)(128)(4,1)} %bitcast.79), calls=%async_computation.6 | async-start | bytes 786432 | tf_op jit(solution)/shard_map/while
  203.9 2.4 copy-start
  203.9 2.4 copy-start.1
  227.5 5.5 %copy-start.3 = (f32[1024]{0:T(1024)S(1)}, f32[1024]{0:T(1024)}, u32[]{:S(2)}) copy-start(f32[1024]{0:T(1024)} %param.11) | copy-start | bytes 12292
Sparse Core Ops, SparseCore 0:
  55.2 91.1 all-gather.2
